TPU v7x, 256 devices: a whole 4x4x8 slice. The times are simulated.
256 devices in a mesh: group: 32 (over z, y), tensor: 8 (over x, core).
Axes of the slice: x: 4, y: 4, z: 8, core: 2. Of those that a mesh axis runs over, the one named last changes fastest.
Arguments:
- query: bfloat16 [2, 1024, 2048], P(None, 'group', 'tensor'), may hold values from -80 to 80
- self_kv: bfloat16 [2, 1024, 2, 2048], P(None, 'group', None, 'tensor'), may hold values from -6 to 6
- kv_pages: bfloat16 [2, 1536, 16, 2, 2048], P(None, 'group', None, None, 'tensor'), may hold values from -6 to 6
- page_dest: int32 [1536, 1], replicated, may hold values from 0 to 31; in each aligned block of 48 rows (0 to 47, 48 to 95, ...) at most 3 rows name the same one
- page_request: int32 [1536], replicated, may hold values from 0 to 1
- score_len: int32 [64], P('group'), may hold values from 1 to 16
- out_proj: bfloat16 [2, 2048, 2048], P(None, 'tensor'), may hold values from -0.125 to 0.125
- residual: bfloat16 [2, 1024, 2048], P(None, ('group', 'tensor')), may hold values from -6 to 6
- norm_gain: float32 [2, 2048], replicated, may hold values from 0.5 to 40
- norm_bias: float32 [2, 2048], replicated, may hold values from -3 to 3
- vocab: bfloat16 [2, 2048, 196608], P(None, None, ('group', 'tensor')), may hold values from -0.3984375 to 0.3984375
- targets: int32 [1024], replicated, may hold values from 0 to 196607
Outputs:
- logprob: float32 [2, 1024], P(None, ('group', 'tensor'))
Inputs may be any that keep to these rules, and one draw needn't show every extreme that they name: `page_dest`: the 48 pages of each aligned block (pages held by one group) go to any one group at most 3 times; some block sends exactly 3 to some group.
All inputs are finite; a program needn't handle non-finite values.
Results may differ from a plain program's by a relative error of at most 0.00097.
Values may be sent and summed in bfloat16 or wider, within the bound.
No kernel may reach another device: no remote copies, remote signals or barrier semaphores. Data moves between devices by JAX's collectives and lax.ppermute only.
A program may use at most 128 MiB of HBM per device.

v0:
```python
import math
import jax
import jax.numpy as jnp
from jax import lax
from jax.sharding import PartitionSpec as P

HEADS = 16
HEAD_DIM = 128
REQ_GRP = 2
SCORE_LEN = 16
NEGATIVE = -1e30
EPSILON = 1e-05


def alibi_slopes(head_count):
    return jnp.exp2(-8.0 * jnp.arange(1, head_count + 1).astype(jnp.float32) / head_count)


def lse_combine(peak, total, chosen, axis):
    top = jnp.max(peak, axis=axis, keepdims=True)
    total = jnp.sum(total * jnp.exp(peak - top), axis=axis)
    return (jnp.squeeze(top, axis), total, jnp.sum(chosen, axis=axis))


def per_device(
    query,
    self_kv,
    kv_pages,
    page_dest,
    page_request,
    score_len,
    out_proj,
    residual,
    norm_gain,
    norm_bias,
    vocab,
    targets,
):
    groups = lax.axis_size("group")
    shards = lax.axis_size("tensor")
    group_id = lax.axis_index("group")
    tensor_id = lax.axis_index("tensor")
    tok_grp = query.shape[1]
    flat_width = query.shape[2]
    head_local = flat_width // HEAD_DIM
    per_owner = kv_pages.shape[1]
    page_len = kv_pages.shape[2]
    capacity = 2 * per_owner // groups
    destination = page_dest[:, 0]
    page_total = destination.shape[0]
    buffer = groups * capacity
    width = residual.shape[2]
    local = jnp.arange(per_owner, dtype=jnp.int32)
    earlier = local[None, :] < local[:, None]
    my_dest = lax.dynamic_slice_in_dim(destination, group_id * per_owner, per_owner)
    my_position = jnp.sum(
        ((my_dest[None, :] == my_dest[:, None]) & earlier).astype(jnp.int32), axis=1
    )
    out_slot = my_dest * capacity + my_position
    slots = jnp.arange(buffer, dtype=jnp.int32)
    send_hot = out_slot[None, :] == slots[:, None]
    send_from = jnp.sum(jnp.where(send_hot, local[None, :], 0), axis=1)
    outgoing = jnp.take(kv_pages, send_from, axis=1)
    incoming = lax.all_to_all(outgoing, "group", split_axis=1, concat_axis=1, tiled=True)
    pages = jnp.arange(page_total, dtype=jnp.int32)
    mine = destination == group_id
    mine_blocks = mine.reshape(groups, per_owner)
    rank_in_block = jnp.sum(
        (mine_blocks[:, None, :] & earlier[None]).astype(jnp.int32), axis=2
    ).reshape(-1)
    arrival = pages // per_owner * capacity + rank_in_block
    recv_hot = mine[None, :] & (arrival[None, :] == slots[:, None])
    is_valid = jnp.any(recv_hot, axis=1)
    slot_page = jnp.sum(jnp.where(recv_hot, pages[None, :], 0), axis=1)
    slot_request = jnp.sum(jnp.where(recv_hot, page_request[None, :], 0), axis=1)
    slot_rank = jnp.sum(
        (
            mine[None, :]
            & (page_request[None, :] == slot_request[:, None])
            & (pages[None, :] < slot_page[:, None])
        ).astype(jnp.int32),
        axis=1,
    )
    request_ids = jnp.arange(REQ_GRP, dtype=jnp.int32)
    totals = jnp.sum(
        (mine[None, :] & (page_request[None, :] == request_ids[:, None])).astype(jnp.int32), axis=1
    )
    slopes = lax.dynamic_slice_in_dim(alibi_slopes(HEADS), tensor_id * head_local, head_local)
    score_scale = 1.0 / math.sqrt(HEAD_DIM)
    queries = query.reshape(2, tok_grp, head_local, HEAD_DIM)
    own_keys = self_kv[:, :, 0].reshape(2, tok_grp, head_local, HEAD_DIM)
    own_values = self_kv[:, :, 1].reshape(2, tok_grp, head_local, HEAD_DIM)
    token_ids = jnp.arange(tok_grp, dtype=jnp.int32)
    token_request = token_ids // SCORE_LEN
    token_step = token_ids % SCORE_LEN
    own_distance = (token_step[:, None] - token_step[None, :]).astype(jnp.float32)
    own_scores = (
        jnp.einsum("mthd,mshd->mhts", queries, own_keys, preferred_element_type=jnp.float32)
        * score_scale
    )
    own_scores = own_scores - slopes[None, :, None, None] * own_distance[None, None]
    own_allowed = (
        (token_request[:, None] == token_request[None, :])
        & (token_step[None, :] <= token_step[:, None])
    )[None, None]
    own_scores = jnp.where(own_allowed, own_scores, NEGATIVE)
    own_top = jnp.max(own_scores, -1)
    key_data = incoming[:, :, :, 0].reshape(2, buffer * page_len, head_local, HEAD_DIM)
    values = incoming[:, :, :, 1].reshape(2, buffer * page_len, head_local, HEAD_DIM)
    key_request = jnp.repeat(jnp.where(is_valid, slot_request, -1), page_len)
    key_position = (
        slot_rank[:, None] * page_len + jnp.arange(page_len, dtype=jnp.int32)[None, :]
    ).reshape(-1)
    context = totals[token_request] * page_len
    distance = ((context + token_step)[:, None] - key_position[None, :]).astype(jnp.float32)
    scores = (
        jnp.einsum("mthd,mkhd->mhtk", queries, key_data, preferred_element_type=jnp.float32)
        * score_scale
    )
    scores = scores - slopes[None, :, None, None] * distance[None, None]
    allowed = (key_request[None, :] == token_request[:, None])[None, None]
    scores = jnp.where(allowed, scores, NEGATIVE)
    row_top = jnp.maximum(jnp.max(scores, -1), own_top)
    exp_terms = jnp.where(allowed, jnp.exp(scores - row_top[..., None]), 0.0)
    denominator = jnp.sum(exp_terms, -1)
    numerator = jnp.einsum(
        "mhtk,mkhd->mthd",
        exp_terms.astype(jnp.bfloat16),
        values,
        preferred_element_type=jnp.float32,
    )
    own_terms = jnp.where(own_allowed, jnp.exp(own_scores - row_top[..., None]), 0.0)
    denominator = denominator + jnp.sum(own_terms, -1)
    numerator = numerator + jnp.einsum(
        "mhts,mshd->mthd",
        own_terms.astype(jnp.bfloat16),
        own_values,
        preferred_element_type=jnp.float32,
    )
    attended = (
        (numerator / jnp.transpose(denominator, (0, 2, 1))[..., None])
        .reshape(2, tok_grp, flat_width)
        .astype(jnp.bfloat16)
    )
    rows_local = tok_grp // shards
    partial = jnp.einsum("mtk,mkd->tmd", attended, out_proj, preferred_element_type=jnp.float32)
    parts = lax.all_to_all(
        partial.reshape(shards, rows_local, 2, width), "tensor", 0, 0, tiled=True
    )
    mixed = jnp.sum(parts, axis=0)
    hidden = residual.astype(jnp.float32) + jnp.transpose(mixed, (1, 0, 2))
    row_mean = jnp.mean(hidden, axis=-1, keepdims=True)
    centered = hidden - row_mean
    variance = jnp.mean(centered * centered, axis=-1, keepdims=True)
    normed = (
        centered / jnp.sqrt(variance + EPSILON) * norm_gain[:, None, :] + norm_bias[:, None, :]
    ).astype(jnp.bfloat16)
    voc_local = vocab.shape[2]
    offset = (group_id * shards + tensor_id) * voc_local
    everyone = lax.all_gather(normed, ("group", "tensor"), axis=1, tiled=True)
    logits = jnp.einsum("mnd,mdv->mnv", everyone, vocab, preferred_element_type=jnp.float32)
    local_peak = jnp.max(logits, axis=2)
    local_total = jnp.sum(jnp.exp(logits - local_peak[..., None]), axis=2)
    wanted = targets - offset
    hit = jnp.arange(voc_local, dtype=jnp.int32)[None, None, :] == wanted[None, :, None]
    local_chosen = jnp.sum(jnp.where(hit, logits, 0.0), axis=2)
    stats = jnp.stack([local_peak, local_total, local_chosen]).reshape(
        3, 2, groups, shards, rows_local
    )
    stats = lax.all_to_all(stats, "tensor", 3, 3, tiled=True)
    peak, total, chosen = lse_combine(stats[0], stats[1], stats[2], 2)
    stats = lax.all_to_all(jnp.stack([peak, total, chosen]), "group", 2, 2, tiled=True)
    peak, total, chosen = lse_combine(stats[0], stats[1], stats[2], 1)
    mine_lp = chosen - (peak + jnp.log(total))
    local_ids = tensor_id * rows_local + jnp.arange(rows_local, dtype=jnp.int32)
    keep_token = local_ids % SCORE_LEN < score_len[local_ids // SCORE_LEN]
    return jnp.where(keep_token[None, :], mine_lp, 0.0)


def solution(mesh):
    in_specs = (
        P(None, "group", "tensor"),
        P(None, "group", None, "tensor"),
        P(None, "group", None, None, "tensor"),
        P(),
        P(),
        P("group"),
        P(None, "tensor", None),
        P(None, ("group", "tensor"), None),
        P(),
        P(),
        P(None, None, ("group", "tensor")),
        P(),
    )
    out_specs = P(None, ("group", "tensor"))
    return jax.shard_map(
        per_device, mesh=mesh, in_specs=in_specs, out_specs=out_specs, check_vma=False
    )
```

profile of v0, /device:TPU:1, one launch (start us, length us, event | category | flops | bytes accessed | tf_op | source)
XLA Modules:
  0.0 330.0 jit_solution(15946534215800585845)
XLA Ops:
  6.5 0.9 dynamic-slice_bitcast_fusion
  7.6 0.8 multiply_add_fusion
  8.5 10.7 %gather_fusion.1 = bf16[96,2,16,2,256]{4,3,2,1,0:T(2,128)(2,1)} fusion(bf16[2,48,16,2,256]{4,3,2,1,0:T(2,128)(2,1)} %param.14, s32[1024]{0:T(1024)S(1)} %pad_clamp_fusion), kind=kCustom, calls=%fused_computation.1 | custom fusion | bytes 6291840 | tf_op jit(solution)/shard_map/jit(_take)/gather | solution.py:63
  19.2 6.4 %fusion.2 = bf16[2,96,16,2,256]{4,3,2,0,1:T(2,128)(2,1)} fusion(bf16[96,2,16,2,256]{4,3,2,1,0:T(2,128)(2,1)} %gather_fusion.1, pred[96]{0:T(512)(128)(4,1)S(1)} %compare_and_fusion.1), kind=kLoop, calls=%fused_computation.8 | loop fusion | flops 1572864 | bytes 6291552 | tf_op jit(solution)/shard_map/jit(_take)/select_n | solution.py:63
  25.6 12.3 %all-to-all-start = ((bf16[2,96,16,2,256]{4,3,2,0,1:T(2,128)(2,1)}), bf16[2,96,16,2,256]{4,3,2,0,1:T(2,128)(2,1)}, u32[]{:S(2)}, u32[]{:S(2)}) async-start(bf16[2,96,16,2,256]{4,3,2,0,1:T(2,128)(2,1)} %fusion.2), calls=%async_computation | async-start | bytes 6291456 | tf_op jit(solution)/shard_map/all_to_all | solution.py:64
  41.0 1.2 fusion.67
  43.2 65.1 %all-to-all-done = bf16[2,96,16,2,256]{4,3,2,0,1:T(2,128)(2,1)} async-done(((bf16[2,96,16,2,256]{4,3,2,0,1:T(2,128)(2,1)}), bf16[2,96,16,2,256]{4,3,2,0,1:T(2,128)(2,1)}, u32[]{:S(2)}, u32[]{:S(2)}) %all-to-all-start) | async-done | bytes 3145760 | tf_op jit(solution)/shard_map/all_to_all | solution.py:64
  108.2 9.8 %fusion.73 = (bf16[2,96,16,1,256]{4,3,2,0,1:T(2,128)(2,1)}, bf16[2,96,16,1,256]{4,3,2,0,1:T(2,128)(2,1)S(1)}) fusion(bf16[2,96,16,2,256]{4,3,2,0,1:T(2,128)(2,1)} %all-to-all-done), kind=kLoop, calls=%fused_computation.145 | loop fusion | bytes 6291456 | tf_op jit(solution)/shard_map/slice | solution.py:109
  118.1 1.6 copy.71
  119.7 3.5 %reshape_squeeze.13 = bf16[2,1536,2,128]{3,2,1,0:T(2,128)(2,1)} reshape(bf16[2,96,16,1,256]{4,2,1,0,3:T(8,128)(2,1)} %copy.71) | data formatting | bytes 3145728 | tf_op jit(solution)/shard_map/reshape;squeeze | solution.py:108
  123.2 2.3 fusion.75
  126.1 1.6 copy.70
  127.7 3.5 %reshape_squeeze.12 = bf16[2,1536,2,128]{3,2,1,0:T(2,128)(2,1)} reshape(bf16[2,96,16,1,256]{4,2,1,0,3:T(8,128)(2,1)} %copy.70) | data formatting | bytes 3145728 | tf_op jit(solution)/shard_map/reshape;squeeze | solution.py:109
  131.2 1.9 fusion.23
  133.8 16.4 %all_to_all.20 = f32[8,4,2,2048]{3,1,2,0:T(4,128)S(1)} all-to-all(f32[8,4,2,2048]{3,1,2,0:T(4,128)S(1)} %copy.80), channel_id=1, replica_groups=mesh['group'=32,'tensor'=8] {'tensor'}, dimensions={0} | all-to-all | bytes 1048576 | tf_op jit(solution)/shard_map/all_to_all | solution.py:147
  152.0 114.4 %all-gather.2.cloned.1.call-done = bf16[2,1024,2048]{2,0,1:T(2,128)(2,1)} async-done(((bf16[2,4,2048]{2,0,1:T(2,128)(2,1)}), bf16[2,1024,2048]{2,0,1:T(2,128)(2,1)}) %all-gather.2.cloned.1.call-update) | async-done | bytes 8388624 | tf_op jit(solution)/shard_map/all_gather | solution.py:160
  266.4 23.1 %fusion.77 = (f32[2,1024]{1,0:T(2,128)S(1)}, f32[2,1024,768]{1,2,0:T(8,128)}) fusion(bf16[2,2048,768]{2,1,0:T(8,128)(2,1)} %param.22, bf16[2,1024,2048]{2,0,1:T(2,128)(2,1)} %all-gather.2.cloned.1.call-done), kind=kOutput, calls=%fused_computation.149 | convolution fusion | flops 6444021760 | bytes 20979712 | tf_op jit(solution)/shard_map/mnd,mdv->mnv/dot_general | solution.py:161
  289.8 3.6 %exponential_reduce_fusion = (f32[2,1024]{1,0:T(2,128)S(1)}, f32[2,1024]{1,0:T(2,128)S(1)}) fusion(f32[2,1024,768]{1,2,0:T(8,128)} %get-tuple-element.20, f32[2,1024]{1,0:T(2,128)S(1)} %get-tuple-element.19, pred[1024,768]{0,1:T(8,128)(4,1)S(1)} %iota_compare_fusion), kind=kLoop, calls=%fused_computation.5 | loop fusion | flops 6287360 | bytes 7102464 | tf_op jit(solution)/shard_map/reduce_sum | solution.py:163
  293.7 1.0 stack.23
  294.7 1.0 pad_maximum_fusion
  296.8 4.3 %all-to-all-start.2 = ((f32[8,1,768]{2,1,0:T(1,128)}), f32[8,1,768]{2,1,0:T(1,128)S(1)}, u32[]{:S(2)}, u32[]{:S(2)}) async-start(f32[8,1,768]{2,1,0:T(1,128)} %reshape.516), calls=%async_computation.2 | async-start | bytes 49152 | tf_op jit(solution)/shard_map/all_to_all | solution.py:170
  301.8 4.0 %all-to-all-done.2 = f32[8,1,768]{2,1,0:T(1,128)S(1)} async-done(((f32[8,1,768]{2,1,0:T(1,128)}), f32[8,1,768]{2,1,0:T(1,128)S(1)}, u32[]{:S(2)}, u32[]{:S(2)}) %all-to-all-start.2) | async-done | bytes 24608 | tf_op jit(solution)/shard_map/all_to_all | solution.py:170
  308.0 5.4 %all-to-all-start.3 = ((f32[3,2,32,4]{3,1,0,2:T(2,128)}), f32[3,2,32,4]{3,1,0,2:T(2,128)S(1)}, u32[]{:S(2)}, u32[]{:S(2)}) async-start(f32[3,2,32,4]{3,1,0,2:T(2,128)} %copy.86), calls=%async_computation.3 | async-start | bytes 196608 | tf_op jit(solution)/shard_map/all_to_all | solution.py:172
  313.4 9.1 %all-to-all-done.3 = f32[3,2,32,4]{3,1,0,2:T(2,128)S(1)} async-done(((f32[3,2,32,4]{3,1,0,2:T(2,128)}), f32[3,2,32,4]{3,1,0,2:T(2,128)S(1)}, u32[]{:S(2)}, u32[]{:S(2)}) %all-to-all-start.3) | async-done | bytes 3104 | tf_op jit(solution)/shard_map/all_to_all | solution.py:172
  (94 shorter events, 12.4 us)
Async XLA Ops:
  6.5 126.6 %copy-start = (bf16[2,256,2048]{2,1,0:T(8,128)(2,1)S(1)}, bf16[2,256,2048]{2,1,0:T(8,128)(2,1)}, u32[]{:S(2)}) copy-start(bf16[2,256,2048]{2,1,0:T(8,128)(2,1)} %param.18) | copy-start | bytes 6291460
  25.6 12.5 %copy-start.9 = (s32[1536,1]{0,1:T(1,128)S(1)}, s32[1536,1]{0,1:T(1,128)}, u32[]{:S(2)}) copy-start(s32[1536,1]{0,1:T(1,128)} %param.15) | copy-start | bytes 18436
  25.6 13.4 %copy-start.5 = (s32[1536]{0:T(1024)S(1)}, s32[1536]{0:T(1024)}, u32[]{:S(2)}) copy-start(s32[1536]{0:T(1024)} %param.16) | copy-start | bytes 18436
  25.6 16.6 %copy-start.4 = (bf16[2,32,2,256]{3,2,1,0:T(2,128)(2,1)S(1)}, bf16[2,32,2,256]{3,2,1,0:T(2,128)(2,1)}, u32[]{:S(2)}) copy-start(bf16[2,32,2,256]{3,2,1,0:T(2,128)(2,1)} %param.13) | copy-start | bytes 196612
  25.6 17.1 %copy-start.6 = (bf16[2,32,256]{2,1,0:T(8,128)(2,1)S(1)}, bf16[2,32,256]{2,1,0:T(8,128)(2,1)}, u32[]{:S(2)}) copy-start(bf16[2,32,256]{2,1,0:T(8,128)(2,1)} %param.12) | copy-start | bytes 98308
  25.6 82.6 %all-to-all-start = ((bf16[2,96,16,2,256]{4,3,2,0,1:T(2,128)(2,1)}), bf16[2,96,16,2,256]{4,3,2,0,1:T(2,128)(2,1)}, u32[]{:S(2)}, u32[]{:S(2)}) async-start(bf16[2,96,16,2,256]{4,3,2,0,1:T(2,128)(2,1)} %fusion.2), calls=%async_computation | async-start | bytes 6291456 | tf_op jit(solution)/shard_map/all_to_all | solution.py:64
  37.9 228.5 %all-gather.2.cloned.1.call-start = ((), (), s32[]{:S(2)}) async-start(), calls=%async_computation.4 | async-start | bytes 8421376 | tf_op jit(solution)/shard_map/all_gather | solution.py:160
  123.2 2.9 copy-start.2
  133.1 17.2 %copy-start.3 = (bf16[2,4,2048]{2,1,0:T(4,128)(2,1)S(1)}, bf16[2,4,2048]{2,1,0:T(4,128)(2,1)}, u32[]{:S(2)}) copy-start(bf16[2,4,2048]{2,1,0:T(4,128)(2,1)} %param.19) | copy-start | bytes 98308
  133.1 17.5 %copy-start.7 = (f32[2,2048]{1,0:T(2,128)S(1)}, f32[2,2048]{1,0:T(2,128)}, u32[]{:S(2)}) copy-start(f32[2,2048]{1,0:T(2,128)} %param.21) | copy-start | bytes 49156
  133.1 17.5 %copy-start.8 = (f32[2,2048]{1,0:T(2,128)S(1)}, f32[2,2048]{1,0:T(2,128)}, u32[]{:S(2)}) copy-start(f32[2,2048]{1,0:T(2,128)} %param.20) | copy-start | bytes 49156
  133.1 18.3 %copy-start.10 = (s32[1024]{0:T(1024)S(1)}, s32[1024]{0:T(1024)}, u32[]{:S(2)}) copy-start(s32[1024]{0:T(1024)} %param.23) | copy-start | bytes 12292
  293.4 7.7 %copy-start.1 = (s32[2]{0:T(128)S(1)}, s32[2]{0:T(128)}, u32[]{:S(2)}) copy-start(s32[2]{0:T(128)} %param.17) | copy-start | bytes 28
  296.8 9.0 %all-to-all-start.2 = ((f32[8,1,768]{2,1,0:T(1,128)}), f32[8,1,768]{2,1,0:T(1,128)S(1)}, u32[]{:S(2)}, u32[]{:S(2)}) async-start(f32[8,1,768]{2,1,0:T(1,128)} %reshape.516), calls=%async_computation.2 | async-start | bytes 49152 | tf_op jit(solution)/shard_map/all_to_all | solution.py:170
  308.0 14.5 %all-to-all-start.3 = ((f32[3,2,32,4]{3,1,0,2:T(2,128)}), f32[3,2,32,4]{3,1,0,2:T(2,128)S(1)}, u32[]{:S(2)}, u32[]{:S(2)}) async-start(f32[3,2,32,4]{3,1,0,2:T(2,128)} %copy.86), calls=%async_computation.3 | async-start | bytes 196608 | tf_op jit(solution)/shard_map/all_to_all | solution.py:172
Sparse Core Ops, SparseCore 0:
  151.5 114.8 all-gather.1
where the time goes:
time: 331 us; the launch traced here: 330 us
  waiting for transfers between devices  193 us (58%)
  local copies, waits for them, and re-layouts  38.5 us (12%)
  matrix products  28.1 us (8%)
  starting transfers between devices  22.2 us (7%)
  other arithmetic  18.5 us (6%)
  blocking collectives  16.4 us (5%)
  between operations  13.7 us (4%)
    all_gather x1, waiting for transfers between devices, per_device(): everyone = lax.all_gather(normed, ('group', 'tensor'), axis=1, tiled=True)  114 us
    all_to_all x1, waiting for transfers between devices, per_device(): lax.all_to_all(outgoing, 'group', split_axis=1, concat_axis=1, tiled=True)  65.1 us
    dot_general x1, matrix products, per_device(): jnp.einsum('mnd,mdv->mnv', everyone, vocab, preferred_element_type=jnp.fl...  23.1 us
    all_to_all x1, blocking collectives, per_device(): lax.all_to_all(partial.reshape(shards, rows_local, 2, width), 'tensor', 0...  16.4 us
    all_to_all x1, starting transfers between devices, per_device(): lax.all_to_all(outgoing, 'group', split_axis=1, concat_axis=1, tiled=True)  12.3 us
    slice x2, local copies, waits for them, and re-layouts, per_device(): incoming[:, :, :, 1].reshape(2, buffer * page_len, head_local, HEAD_DIM)  11.5 us
    gather x1, local copies, waits for them, and re-layouts, per_device(): outgoing = jnp.take(kv_pages, send_from, axis=1)  10.7 us
    all_to_all x1, waiting for transfers between devices, per_device(): lax.all_to_all(jnp.stack([peak, total, chosen]), 'group', 2, 2, tiled=True)  9.06 us
  transfers between devices with their start and end apart: 4, of which 4 were waited for; matrix products, arithmetic and copies ran while one was open for 2% of the time, Pallas kernels for 0%

commit v1 on v0

--- a/solution.py
+++ b/solution.py
@@ -157,7 +157,12 @@
     ).astype(jnp.bfloat16)
     voc_local = vocab.shape[2]
     offset = (group_id * shards + tensor_id) * voc_local
-    everyone = lax.all_gather(normed, ("group", "tensor"), axis=1, tiled=True)
+    everyone = jnp.concatenate(
+        lax.all_to_all(
+            jnp.stack([normed] * lax.axis_size(("group", "tensor"))), ("group", "tensor"), 0, 0
+        ),
+        axis=1,
+    )
     logits = jnp.einsum("mnd,mdv->mnv", everyone, vocab, preferred_element_type=jnp.float32)
     local_peak = jnp.max(logits, axis=2)
     local_total = jnp.sum(jnp.exp(logits - local_peak[..., None]), axis=2)

time: 331 us -> 416 us (1.26)
  waiting for transfers between devices: 193 us -> 263 us
  local copies, waits for them, and re-layouts: 38.5 us -> 66.3 us
  between operations: 13.7 us -> 0.36 us
  matrix products: 28.1 us -> 17.8 us
  starting transfers between devices: 22.2 us -> 32.3 us
    all_to_all x0 -> x1, waiting for transfers between devices: none -> 185 us  [per_device(): lax.all_to_all(jnp.stack([normed] * lax.axis_size(('group', 'tensor'))),...]
    all_gather x1 -> x0, waiting for transfers between devices: 114 us -> none  [per_device(): everyone = lax.all_gather(normed, ('group', 'tensor'), axis=1, tiled=True)]
    reshape x0 -> x2, local copies, waits for them, and re-layouts: none -> 20.9 us  [per_device(): jnp.concatenate(lax.all_to_all(jnp.stack([normed] * lax.axis_size(('group...]
    dot_general x1, matrix products: 23.1 us -> 12.9 us  [per_device(): jnp.einsum('mnd,mdv->mnv', everyone, vocab, preferred_element_type=jnp.fl...]
    all_to_all x0 -> x1, starting transfers between devices: none -> 9.15 us  [per_device(): lax.all_to_all(jnp.stack([normed] * lax.axis_size(('group', 'tensor'))),...]
    another operation x0 -> x1, local copies, waits for them, and re-layouts: none -> 7.49 us  [per_device(): jnp.stack([normed] * lax.axis_size(('group', 'tensor')))]
  transfers between devices with their start and end apart: 4 -> 4, of which waited for: 4 -> 4; matrix products, arithmetic and copies ran while one was open for 2% -> 1% of each run, Pallas kernels for 0% -> 0%
where the time goes in v1:
time: 416 us; the launch traced here: 415 us
  waiting for transfers between devices  263 us (63%)
  local copies, waits for them, and re-layouts  66.3 us (16%)
  starting transfers between devices  32.3 us (8%)
  other arithmetic  18.6 us (4%)
  matrix products  17.8 us (4%)
  blocking collectives  16 us (4%)
    all_to_all x1, waiting for transfers between devices, per_device(): lax.all_to_all(jnp.stack([normed] * lax.axis_size(('group', 'tensor'))),...  185 us
    all_to_all x1, waiting for transfers between devices, per_device(): lax.all_to_all(outgoing, 'group', split_axis=1, concat_axis=1, tiled=True)  65.5 us
    reshape x2, local copies, waits for them, and re-layouts, per_device(): jnp.concatenate(lax.all_to_all(jnp.stack([normed] * lax.axis_size(('group...  20.9 us
    all_to_all x1, blocking collectives, per_device(): lax.all_to_all(partial.reshape(shards, rows_local, 2, width), 'tensor', 0...  16 us
    dot_general x1, matrix products, per_device(): jnp.einsum('mnd,mdv->mnv', everyone, vocab, preferred_element_type=jnp.fl...  12.9 us
    all_to_all x1, starting transfers between devices, per_device(): lax.all_to_all(outgoing, 'group', split_axis=1, concat_axis=1, tiled=True)  12.5 us
    slice x2, local copies, waits for them, and re-layouts, per_device(): incoming[:, :, :, 1].reshape(2, buffer * page_len, head_local, HEAD_DIM)  11.5 us
    gather x1, local copies, waits for them, and re-layouts, per_device(): outgoing = jnp.take(kv_pages, send_from, axis=1)  10.7 us
  transfers between devices with their start and end apart: 4, of which 4 were waited for; matrix products, arithmetic and copies ran while one was open for 1% of the time, Pallas kernels for 0%

profile of v1, /device:TPU:1, one launch (start us, length us, event | category | flops | bytes accessed | tf_op | source)
XLA Modules:
  0.0 414.8 jit_solution(9609983666114317429)
XLA Ops:
  2.0 10.7 %gather_fusion.1 = bf16[96,2,16,2,256]{4,3,2,1,0:T(2,128)(2,1)} fusion(bf16[2,48,16,2,256]{4,3,2,1,0:T(2,128)(2,1)} %param.14, s32[1024]{0:T(1024)S(1)} %pad_clamp_fusion), kind=kCustom, calls=%fused_computation.1 | custom fusion | bytes 6291840 | tf_op jit(solution)/shard_map/jit(_take)/gather | solution.py:63
  12.7 6.4 %fusion = bf16[2,96,16,2,256]{4,3,2,0,1:T(2,128)(2,1)} fusion(bf16[96,2,16,2,256]{4,3,2,1,0:T(2,128)(2,1)} %gather_fusion.1, pred[96]{0:T(512)(128)(4,1)S(1)} %compare_and_fusion.1), kind=kLoop, calls=%fused_computation.6 | loop fusion | flops 1572864 | bytes 6291552 | tf_op jit(solution)/shard_map/jit(_take)/select_n | solution.py:63
  19.1 12.5 %all-to-all-start = ((bf16[2,96,16,2,256]{4,3,2,0,1:T(2,128)(2,1)}), bf16[2,96,16,2,256]{4,3,2,0,1:T(2,128)(2,1)}, u32[]{:S(2)}, u32[]{:S(2)}) async-start(bf16[2,96,16,2,256]{4,3,2,0,1:T(2,128)(2,1)} %fusion), calls=%async_computation | async-start | bytes 6291456 | tf_op jit(solution)/shard_map/all_to_all | solution.py:64
  34.4 1.2 fusion.65
  36.6 65.5 %all-to-all-done = bf16[2,96,16,2,256]{4,3,2,0,1:T(2,128)(2,1)} async-done(((bf16[2,96,16,2,256]{4,3,2,0,1:T(2,128)(2,1)}), bf16[2,96,16,2,256]{4,3,2,0,1:T(2,128)(2,1)}, u32[]{:S(2)}, u32[]{:S(2)}) %all-to-all-start) | async-done | bytes 3145760 | tf_op jit(solution)/shard_map/all_to_all | solution.py:64
  102.1 9.8 %fusion.71 = (bf16[2,96,16,1,256]{4,3,2,0,1:T(2,128)(2,1)}, bf16[2,96,16,1,256]{4,3,2,0,1:T(2,128)(2,1)S(1)}) fusion(bf16[2,96,16,2,256]{4,3,2,0,1:T(2,128)(2,1)} %all-to-all-done), kind=kLoop, calls=%fused_computation.143 | loop fusion | bytes 6291456 | tf_op jit(solution)/shard_map/slice | solution.py:109
  111.9 1.6 copy.49
  113.5 3.5 reshape_squeeze.13
  117.1 2.3 fusion.73
  119.9 1.6 copy.48
  121.6 3.5 reshape_squeeze.12
  125.1 1.9 fusion.21
  127.7 16.0 %all_to_all.25 = f32[8,4,2,2048]{3,1,2,0:T(4,128)S(1)} all-to-all(f32[8,4,2,2048]{3,1,2,0:T(4,128)S(1)} %copy.58), channel_id=1, replica_groups=mesh['group'=32,'tensor'=8] {'tensor'}, dimensions={0} | all-to-all | bytes 1048576 | tf_op jit(solution)/shard_map/all_to_all | solution.py:147
  144.2 7.5 %stack.16 = bf16[256,2,4,2048]{3,2,1,0:T(4,128)(2,1)} broadcast(bf16[2,4,2048]{2,1,0:T(4,128)(2,1)S(1)} %add_convert_fusion), dimensions={1,2,3} | broadcast | bytes 8421376 | tf_op jit(solution)/shard_map/stack | solution.py:162
  151.7 9.1 %all-to-all-start.2 = ((bf16[256,2,4,2048]{3,2,1,0:T(4,128)(2,1)}), bf16[256,2,4,2048]{3,2,1,0:T(4,128)(2,1)}, u32[]{:S(2)}, u32[]{:S(2)}) async-start(bf16[256,2,4,2048]{3,2,1,0:T(4,128)(2,1)} %stack.16), calls=%async_computation.2 | async-start | bytes 16777216 | tf_op jit(solution)/shard_map/all_to_all | solution.py:161
  161.4 184.9 %all-to-all-done.2 = bf16[256,2,4,2048]{3,2,1,0:T(4,128)(2,1)} async-done(((bf16[256,2,4,2048]{3,2,1,0:T(4,128)(2,1)}), bf16[256,2,4,2048]{3,2,1,0:T(4,128)(2,1)}, u32[]{:S(2)}, u32[]{:S(2)}) %all-to-all-start.2) | async-done | bytes 8388640 | tf_op jit(solution)/shard_map/all_to_all | solution.py:161
  346.3 8.4 %copy.59 = bf16[2,256,4,2048]{3,2,1,0:T(4,128)(2,1)} copy(bf16[2,256,4,2048]{3,2,0,1:T(4,128)(2,1)} %bitcast.14) | data formatting | bytes 16777216 | tf_op jit(solution)/shard_map/reshape | solution.py:160
  354.7 12.5 %reshape.487 = bf16[2,1024,2048]{2,1,0:T(8,128)(2,1)} reshape(bf16[2,256,4,2048]{3,2,1,0:T(4,128)(2,1)} %copy.59) | data formatting | bytes 16777216 | tf_op jit(solution)/shard_map/reshape | solution.py:160
  367.2 12.9 %fusion.75 = (f32[2,1024]{1,0:T(2,128)S(1)}, f32[2,1024,768]{1,2,0:T(8,128)}) fusion(bf16[2,1024,2048]{2,1,0:T(8,128)(2,1)} %reshape.487, bf16[2,2048,768]{2,1,0:T(8,128)(2,1)} %param.22), kind=kOutput, calls=%fused_computation.147 | convolution fusion | flops 6444021760 | bytes 20979712 | tf_op jit(solution)/shard_map/mnd,mdv->mnv/dot_general | solution.py:166
  380.4 3.8 exponential_reduce_fusion
  387.5 5.4 %all-to-all-start.3 = ((f32[8,1,768]{2,1,0:T(1,128)}), f32[8,1,768]{2,1,0:T(1,128)S(1)}, u32[]{:S(2)}, u32[]{:S(2)}) async-start(f32[8,1,768]{2,1,0:T(1,128)} %reshape.526), calls=%async_computation.3 | async-start | bytes 49152 | tf_op jit(solution)/shard_map/all_to_all | solution.py:175
  393.6 4.0 all-to-all-done.3
  399.8 5.2 %all-to-all-start.4 = ((f32[3,2,32,4]{3,1,0,2:T(2,128)}), f32[3,2,32,4]{3,1,0,2:T(2,128)S(1)}, u32[]{:S(2)}, u32[]{:S(2)}) async-start(f32[3,2,32,4]{3,1,0,2:T(2,128)} %copy.63), calls=%async_computation.4 | async-start | bytes 196608 | tf_op jit(solution)/shard_map/all_to_all | solution.py:177
  405.1 9.1 %all-to-all-done.4 = f32[3,2,32,4]{3,1,0,2:T(2,128)S(1)} async-done(((f32[3,2,32,4]{3,1,0,2:T(2,128)}), f32[3,2,32,4]{3,1,0,2:T(2,128)S(1)}, u32[]{:S(2)}, u32[]{:S(2)}) %all-to-all-start.4) | async-done | bytes 3104 | tf_op jit(solution)/shard_map/all_to_all | solution.py:177
  (97 shorter events, 15.1 us)
Async XLA Ops:
  0.0 126.9 %copy-start = (bf16[2,256,2048]{2,1,0:T(8,128)(2,1)S(1)}, bf16[2,256,2048]{2,1,0:T(8,128)(2,1)}, u32[]{:S(2)}) copy-start(bf16[2,256,2048]{2,1,0:T(8,128)(2,1)} %param.18) | copy-start | bytes 6291460
  19.1 12.5 %copy-start.10 = (s32[1536,1]{0,1:T(1,128)S(1)}, s32[1536,1]{0,1:T(1,128)}, u32[]{:S(2)}) copy-start(s32[1536,1]{0,1:T(1,128)} %param.15) | copy-start | bytes 18436
  19.1 13.4 %copy-start.6 = (s32[1536]{0:T(1024)S(1)}, s32[1536]{0:T(1024)}, u32[]{:S(2)}) copy-start(s32[1536]{0:T(1024)} %param.16) | copy-start | bytes 18436
  19.1 16.5 %copy-start.5 = (bf16[2,32,2,256]{3,2,1,0:T(2,128)(2,1)S(1)}, bf16[2,32,2,256]{3,2,1,0:T(2,128)(2,1)}, u32[]{:S(2)}) copy-start(bf16[2,32,2,256]{3,2,1,0:T(2,128)(2,1)} %param.13) | copy-start | bytes 196612
  19.1 17.0 %copy-start.7 = (bf16[2,32,256]{2,1,0:T(8,128)(2,1)S(1)}, bf16[2,32,256]{2,1,0:T(8,128)(2,1)}, u32[]{:S(2)}) copy-start(bf16[2,32,256]{2,1,0:T(8,128)(2,1)} %param.12) | copy-start | bytes 98308
  19.1 83.0 %all-to-all-start = ((bf16[2,96,16,2,256]{4,3,2,0,1:T(2,128)(2,1)}), bf16[2,96,16,2,256]{4,3,2,0,1:T(2,128)(2,1)}, u32[]{:S(2)}, u32[]{:S(2)}) async-start(bf16[2,96,16,2,256]{4,3,2,0,1:T(2,128)(2,1)} %fusion), calls=%async_computation | async-start | bytes 6291456 | tf_op jit(solution)/shard_map/all_to_all | solution.py:64
  117.0 2.9 copy-start.3
  126.9 16.8 %copy-start.4 = (bf16[2,4,2048]{2,1,0:T(4,128)(2,1)S(1)}, bf16[2,4,2048]{2,1,0:T(4,128)(2,1)}, u32[]{:S(2)}) copy-start(bf16[2,4,2048]{2,1,0:T(4,128)(2,1)} %param.19) | copy-start | bytes 98308
  127.0 17.1 %copy-start.8 = (f32[2,2048]{1,0:T(2,128)S(1)}, f32[2,2048]{1,0:T(2,128)}, u32[]{:S(2)}) copy-start(f32[2,2048]{1,0:T(2,128)} %param.21) | copy-start | bytes 49156
  127.0 17.1 %copy-start.9 = (f32[2,2048]{1,0:T(2,128)S(1)}, f32[2,2048]{1,0:T(2,128)}, u32[]{:S(2)}) copy-start(f32[2,2048]{1,0:T(2,128)} %param.20) | copy-start | bytes 49156
  151.7 9.2 %copy-start.11 = (s32[1024]{0:T(1024)S(1)}, s32[1024]{0:T(1024)}, u32[]{:S(2)}) copy-start(s32[1024]{0:T(1024)} %param.23) | copy-start | bytes 12292
  151.7 194.7 %all-to-all-start.2 = ((bf16[256,2,4,2048]{3,2,1,0:T(4,128)(2,1)}), bf16[256,2,4,2048]{3,2,1,0:T(4,128)(2,1)}, u32[]{:S(2)}, u32[]{:S(2)}) async-start(bf16[256,2,4,2048]{3,2,1,0:T(4,128)(2,1)} %stack.16), calls=%async_computation.2 | async-start | bytes 16777216 | tf_op jit(solution)/shard_map/all_to_all | solution.py:161
  380.4 34.5 %copy-start.1 = (bf16[2,256,2048]{2,1,0:T(8,128)(2,1)S(1)}, bf16[2,256,2048]{2,1,0:T(8,128)(2,1)}, u32[]{:S(2)}) copy-start(bf16[2,256,2048]{2,1,0:T(8,128)(2,1)} %param.18) | copy-start | bytes 6291460
  384.1 8.8 %copy-start.2 = (s32[2]{0:T(128)S(1)}, s32[2]{0:T(128)}, u32[]{:S(2)}) copy-start(s32[2]{0:T(128)} %param.17) | copy-start | bytes 28
  387.5 10.1 %all-to-all-start.3 = ((f32[8,1,768]{2,1,0:T(1,128)}), f32[8,1,768]{2,1,0:T(1,128)S(1)}, u32[]{:S(2)}, u32[]{:S(2)}) async-start(f32[8,1,768]{2,1,0:T(1,128)} %reshape.526), calls=%async_computation.3 | async-start | bytes 49152 | tf_op jit(solution)/shard_map/all_to_all | solution.py:175
  399.8 14.3 %all-to-all-start.4 = ((f32[3,2,32,4]{3,1,0,2:T(2,128)}), f32[3,2,32,4]{3,1,0,2:T(2,128)S(1)}, u32[]{:S(2)}, u32[]{:S(2)}) async-start(f32[3,2,32,4]{3,1,0,2:T(2,128)} %copy.63), calls=%async_computation.4 | async-start | bytes 196608 | tf_op jit(solution)/shard_map/all_to_all | solution.py:177
